TPU v7x, 32 devices: a whole 2x2x4 slice. The times are simulated.
32 devices in a mesh: section: 4 (over z), dp: 8 (over y, x, core).
Axes of the slice: x: 2, y: 2, z: 4, core: 2. Of those that a mesh axis runs over, the one named last changes fastest.
Arguments:
- layer_inputs: bfloat16 [4, 8, 128, 2560], P('section', 'dp'), may hold values from -6 to 6
- w_bc: bfloat16 [4, 2560, 256], P('section'), may hold values from -0.125 to 0.125
- log_decay: float32 [4, 8, 128, 40], P('section', 'dp'), may hold values from -1.7 to 0, as said below
- top_grad: bfloat16 [8, 128, 2560], P('dp'), may hold values from -6 to 6
Outputs:
- grad_inputs: bfloat16 [4, 8, 128, 2560], P('section', 'dp')
- grad_w: float32 [4, 2560, 256], P('section', 'dp')
Inputs may be any that keep to these rules, and one draw needn't show every extreme that they name: `log_decay`: every entry is negative.
All inputs are finite; a program needn't handle non-finite values.
Results may differ from a plain program's by a relative error of at most 0.0085.
Values may be sent and summed in bfloat16 or wider, within the bound.
No kernel may reach another device: no remote copies, remote signals or barrier semaphores. Data moves between devices by JAX's collectives and lax.ppermute only.
A program may use at most 64 MiB of HBM per device.

v0:
```python
import jax
import jax.numpy as jnp
from jax import lax
from jax.sharding import PartitionSpec as P

MICRO = 4


def shortened(value):
    return jax.tree.map(lambda a: a.astype(jnp.bfloat16) if a.dtype == jnp.float32 else a, value)


def passed_along(block, axis, distance):
    devices = range(lax.axis_size(axis))
    route = [(i - distance, i) for i in devices if i - distance in devices]
    return lax.ppermute(block, axis, route)


def block_terms(inputs_b, in_b, out_b, rates, grads_b, carried, state_in, factor):
    length = inputs_b.shape[0]
    cumulative = jnp.cumsum(rates, axis=0)
    ending = cumulative[-1]
    locations = jnp.arange(length)
    lower_mask = (locations[:, None] >= locations[None, :])[:, :, None]
    spread = jnp.where(lower_mask, cumulative[:, None, :] - cumulative[None, :, :], 0.0)
    decays = jnp.where(lower_mask, jnp.exp(spread), 0.0)
    tail_decay = jnp.exp(ending[None, :] - cumulative)
    leading = jnp.exp(cumulative)
    scores = jnp.dot(out_b, in_b.T, preferred_element_type=jnp.float32)
    weighted = (factor * decays * scores[:, :, None]).astype(jnp.bfloat16)
    carried_b = carried.astype(jnp.bfloat16)
    state_b = state_in.astype(jnp.bfloat16)
    grad_feats = jnp.einsum("kjh,khp->jhp", weighted, grads_b, preferred_element_type=jnp.float32)
    grad_feats = grad_feats + tail_decay[:, :, None] * jnp.einsum(
        "hpn,jn->jhp", carried_b, in_b, preferred_element_type=jnp.float32
    )
    pair_dots = jnp.einsum("khp,jhp->kjh", grads_b, inputs_b, preferred_element_type=jnp.float32)
    mixing = jnp.sum(decays * pair_dots, axis=2).astype(jnp.bfloat16)
    tail_inputs = (tail_decay[:, :, None] * inputs_b.astype(jnp.float32)).astype(jnp.bfloat16)
    lead_grads = (leading[:, :, None] * grads_b.astype(jnp.float32)).astype(jnp.bfloat16)
    grad_inmap = factor * jnp.dot(mixing.T, out_b, preferred_element_type=jnp.float32)
    grad_inmap = grad_inmap + jnp.einsum(
        "jhp,hpn->jn", tail_inputs, carried_b, preferred_element_type=jnp.float32
    )
    grad_outmap = factor * (
        jnp.dot(mixing, in_b, preferred_element_type=jnp.float32)
        + jnp.einsum("ihp,hpn->in", lead_grads, state_b, preferred_element_type=jnp.float32)
    )
    carry_out = factor * jnp.einsum(
        "khp,kn->hpn", lead_grads, out_b, preferred_element_type=jnp.float32
    )
    carry_out = carry_out + jnp.exp(ending)[:, None, None] * carried
    return (grad_feats, grad_inmap, grad_outmap, carry_out)


def block_end(inputs_b, in_b, rates, state_in):
    cumulative = jnp.cumsum(rates, axis=0)
    ending = cumulative[-1]
    tail_decay = jnp.exp(ending[None, :] - cumulative)
    tail_inputs = (tail_decay[:, :, None] * inputs_b.astype(jnp.float32)).astype(jnp.bfloat16)
    fresh = jnp.einsum("jhp,jn->hpn", tail_inputs, in_b, preferred_element_type=jnp.float32)
    return jnp.exp(ending)[:, None, None] * state_in + fresh


def split_block(inputs_c, map_block, head_count):
    length, features = inputs_c.shape
    state_size = map_block.shape[1] // 2
    inputs_b = inputs_c.reshape(length, head_count, features // head_count)
    in_b = map_block[:, :state_size]
    out_b = map_block[:, state_size:]
    return (inputs_b, in_b, out_b)


def block_back(inputs_c, map_block, rates, grads_c, carried, state_in, weights):
    length, features = inputs_c.shape
    head_count = rates.shape[1]
    factor = 0.25 / (map_block.shape[1] // 2)
    inputs_b, in_b, out_b = split_block(inputs_c, map_block, head_count)
    grads_b = grads_c.reshape(length, head_count, features // head_count)
    grad_feats, grad_inmap, grad_outmap, carry_out = block_terms(
        inputs_b, in_b, out_b, rates, grads_b, carried, state_in, factor
    )
    grad_bc = jnp.concatenate([grad_inmap, grad_outmap], axis=1).astype(jnp.bfloat16)
    back_proj = lax.dot_general(
        grad_bc, weights, (((1,), (1,)), ((), ())), preferred_element_type=jnp.float32
    )
    summed = grads_c.astype(jnp.float32) + grad_feats.reshape(length, features) + back_proj
    return (summed.astype(jnp.bfloat16), carry_out, grad_bc)


def layer_starts(inputs_s, bc_s, rates_s):
    head_count = rates_s.shape[1]
    features = inputs_s.shape[1]
    state_size = bc_s.shape[1] // 2
    block_len = inputs_s.shape[0] // MICRO
    state_now = jnp.zeros((head_count, features // head_count, state_size), jnp.float32)
    saved = []
    for block_no in range(MICRO):
        lo_row = block_no * block_len
        inputs_b, in_b, out_b = split_block(
            inputs_s[lo_row : lo_row + block_len], bc_s[lo_row : lo_row + block_len], head_count
        )
        saved.append(state_now)
        state_now = block_end(inputs_b, in_b, rates_s[lo_row : lo_row + block_len], state_now)
    return jnp.stack(saved)


def shards(layer_inputs, w_bc, log_decay, top_grad):
    sections = lax.axis_size("section")
    section_id = lax.axis_index("section")
    lay_dev, seq_dev, tok_len, features = layer_inputs.shape
    block_len = tok_len // MICRO
    bc_all = jnp.einsum(
        "lstd,ldc->lstc", layer_inputs, w_bc, preferred_element_type=jnp.float32
    ).astype(jnp.bfloat16)
    starts = jax.vmap(jax.vmap(layer_starts))(layer_inputs, bc_all, log_decay)
    is_top = section_id == sections - 1
    back_all = jax.vmap(block_back, in_axes=(0, 0, 0, 0, 0, 0, None))

    def advance(counter, loop_state):
        incoming, carried, grad_store, map_store = loop_state
        offset = counter - (sections - 1 - section_id)
        is_valid = (offset >= 0) & (offset < MICRO)
        block_no = jnp.clip(MICRO - 1 - offset, 0, MICRO - 1)
        row_start = block_no * block_len
        from_top = lax.dynamic_slice_in_dim(top_grad, row_start, block_len, 1)
        grad_block = jnp.where(is_top, from_top, incoming)

        def compute(stores):
            carried_in, grads_in, maps_in = stores
            current = grad_block
            for level_no in reversed(range(lay_dev)):
                inputs_c = lax.dynamic_slice_in_dim(layer_inputs[level_no], row_start, block_len, 1)
                map_block = lax.dynamic_slice_in_dim(bc_all[level_no], row_start, block_len, 1)
                rates = lax.dynamic_slice_in_dim(log_decay[level_no], row_start, block_len, 1)
                state_in = lax.dynamic_index_in_dim(starts[level_no], block_no, 1, keepdims=False)
                level_grads, carry_out, grad_bc = back_all(
                    inputs_c,
                    map_block,
                    rates,
                    current,
                    carried_in[level_no],
                    state_in,
                    w_bc[level_no],
                )
                carried_in = carried_in.at[level_no].set(carry_out)
                grads_in = grads_in.at[level_no].set(
                    lax.dynamic_update_slice_in_dim(grads_in[level_no], level_grads, row_start, 1)
                )
                maps_in = maps_in.at[level_no].set(
                    lax.dynamic_update_slice_in_dim(maps_in[level_no], grad_bc, row_start, 1)
                )
                current = level_grads
            return (current, (carried_in, grads_in, maps_in))

        def passing(stores):
            return (jnp.zeros_like(grad_block), stores)

        outgoing, updated = lax.cond(is_valid, compute, passing, (carried, grad_store, map_store))
        received = jax.tree.map(
            lambda part, own: part.astype(own.dtype),
            passed_along(shortened(outgoing), "section", -1),
            outgoing,
        )
        return (received, updated[0], updated[1], updated[2])

    initial = (
        jnp.zeros((seq_dev, block_len, features), jnp.bfloat16),
        jnp.zeros((lay_dev,) + starts.shape[1:2] + starts.shape[3:], jnp.float32),
        jnp.zeros(layer_inputs.shape, jnp.bfloat16),
        jnp.zeros(bc_all.shape, jnp.bfloat16),
    )
    final_state = lax.fori_loop(0, MICRO + sections - 1, advance, initial)
    grad_inputs = final_state[2]
    map_store = final_state[3]
    ways = lax.axis_size("dp")
    divisor = ways * seq_dev
    rows_here = layer_inputs.reshape(lay_dev, seq_dev * tok_len, features)
    rows_all = lax.all_to_all(rows_here, "dp", 2, 1, tiled=True)
    maps_here = map_store.reshape(lay_dev, seq_dev * tok_len, map_store.shape[-1])
    maps_all = lax.all_gather(maps_here, "dp", axis=1, tiled=True)
    grad_w = (
        jnp.einsum("lrd,lrc->ldc", rows_all, maps_all, preferred_element_type=jnp.float32) / divisor
    )
    return (grad_inputs, grad_w)


def solution(mesh):
    in_specs = (
        P("section", "dp", None, None),
        P("section", None, None),
        P("section", "dp", None, None),
        P("dp", None, None),
    )
    out_specs = (P("section", "dp", None, None), P("section", "dp", None))
    return jax.shard_map(shards, mesh=mesh, in_specs=in_specs, out_specs=out_specs, check_vma=False)
```

profile of v0, /device:TPU:0, one launch (start us, length us, event | category | flops | bytes accessed | tf_op | source)
XLA Modules:
  0.0 188.5 jit_solution(8316372705247162726)
XLA Ops:
  0.6 2.5 %copy.89 = bf16[1,128,2560]{1,0,2:T(2,128)(2,1)S(1)} copy(bf16[1,128,2560]{2,1,0:T(8,128)(2,1)} %bitcast.43) | data formatting | bytes 1310720 | tf_op jit(solution)/shard_map/reshape | solution.py:178
  3.7 14.3 %reduce.10 = bf16[2560,128]{1,0:T(8,128)(2,1)S(1)} reduce(bf16[2560,1,128]{2,1,0:T(2,128)(2,1)S(1)} %bitcast.178, bf16[]{:T(256)} %broadcast.353), dimensions={1}, to_apply=%bitcast.170.reduce_sub_computation | reduce | bytes 1310722
  18.9 5.2 %all-to-all-start = ((bf16[8,2,20480]{2,1,0:T(2,128)(2,1)}), bf16[8,2,20480]{2,1,0:T(2,128)(2,1)}, u32[]{:S(2)}, u32[]{:S(2)}) async-start(bf16[8,2,20480]{2,1,0:T(2,128)(2,1)} %reshape.676), calls=%async_computation | async-start | bytes 1310720 | tf_op jit(solution)/shard_map/all_to_all | solution.py:179
  28.2 1.4 fusion.61
  31.3 1.9 %pad_maximum_fusion = bf16[1,1,4,40,64,128]{5,4,3,2,1,0:T(8,128)(2,1)} fusion(bf16[1,1,1,40,64,128]{5,4,3,2,1,0:T(8,128)(2,1)S(1)} %fusion.54, f32[1,1,1,40,64,128]{5,4,3,2,1,0:T(8,128)S(1)} %bitcast.177, f32[1,1,1,40,64,128]{5,4,3,2,1,0:T(8,128)S(1)} %bitcast.176, bf16[4]{0:T(256)(128)(2,1)S(1)} %pad.10.clone), kind=kLoop, calls=%fused_computation.78 | loop fusion | flops 3932160 | bytes 5898248 | tf_op jit(solution)/shard_map/vmap(vmap())/stack | solution.py:105
  34.9 139.4 %while.24 = (s32[]{:T(128)}, bf16[1,32,2560]{2,1,0:T(8,128)(2,1)S(1)}, f32[1,1,40,64,128]{4,3,2,1,0:T(8,128)S(1)}, bf16[1,1,128,2560]{3,2,1,0:T(8,128)(2,1)}, bf...) while((s32[]{:T(128)}, ...), condition=%wide.region_8.9_spmd, body=%wide.region_3.8_spmd.sunk | while | flops 140346368 | bytes 17553168 | solution.py:173
  36.3 7.4 %collective-permute-done = bf16[1,32,2560]{2,1,0:T(8,128)(2,1)S(1)} collective-permute-done((bf16[1,32,2560]{2,1,0:T(8,128)(2,1)S(1)}, bf16[1,32,2560]{2,1,0:T(8,128)(2,1)S(1)}, u32[]{:S(2)}, u32[]{:S(2)}) %collective-permute-start) | collective-permute-done | bytes 163872 | tf_op jit(solution)/shard_map/while/body/eval_jaxpr/ppermute | solution.py:16
  45.0 6.4 %collective-permute-done = bf16[1,32,2560]{2,1,0:T(8,128)(2,1)S(1)} collective-permute-done((bf16[1,32,2560]{2,1,0:T(8,128)(2,1)S(1)}, bf16[1,32,2560]{2,1,0:T(8,128)(2,1)S(1)}, u32[]{:S(2)}, u32[]{:S(2)}) %collective-permute-start) | collective-permute-done | bytes 163872 | tf_op jit(solution)/shard_map/while/body/eval_jaxpr/ppermute | solution.py:16
  52.7 42.5 %collective-permute-done = bf16[1,32,2560]{2,1,0:T(8,128)(2,1)S(1)} collective-permute-done((bf16[1,32,2560]{2,1,0:T(8,128)(2,1)S(1)}, bf16[1,32,2560]{2,1,0:T(8,128)(2,1)S(1)}, u32[]{:S(2)}, u32[]{:S(2)}) %collective-permute-start) | collective-permute-done | bytes 163872 | tf_op jit(solution)/shard_map/while/body/eval_jaxpr/ppermute | solution.py:16
  95.2 12.6 %conditional.2 = (bf16[1,32,2560]{2,1,0:T(8,128)(2,1)S(1)}, f32[1,1,40,64,128]{4,3,2,1,0:T(8,128)S(1)}, bf16[1,1,128,2560]{3,2,1,0:T(8,128)(2,1)}, bf16[1,1,128,256]{3,2,1,0:T(8,128)(2,1)}) conditional(s32[]{:T(128)} %convert_element_type.236, (f32[1,1,40,64,128]{4,3,2,1,0:T(8,128)S(1)}, bf16[1,1,128,2560]{3,2,1,0:T(8,128)(2,1)}, ...), branch_computations={%region_4.4_spmd, %region_5.7_spmd} | conditional | flops 140346368 | bytes 16897460 | solution.py:159
  104.6 2.5 %bitcast_dynamic-update-slice_fusion = (bf16[1,1,128,2560]{3,2,1,0:T(8,128)(2,1)}, bf16[1,32,2560]{2,1,0:T(8,128)(2,1)S(1)}) fusion(bf16[1,1,128,2560]{3,2,1,0:T(8,128)(2,1)} %get-tuple-element.483, s32[]{:T(128)S(6)} %select_n.90, bf16[1,2560,256]{2,1,0:T(8,128)(2,1)} %get-tuple-element.482, bf16[32,128]{1,0:T(8,128)(2,1)S(1)} %fusion.13, ...), kind=kOutput, calls=%fused_computation.46 | convolution fusion | flops 42303488 | bytes 2146308 | tf_op jit(solution)/shard_map/while/body/eval_jaxpr/cond/branch_1_fun/vmap()/dot_general | solution.py:84
  109.1 5.9 %collective-permute-done = bf16[1,32,2560]{2,1,0:T(8,128)(2,1)S(1)} collective-permute-done((bf16[1,32,2560]{2,1,0:T(8,128)(2,1)S(1)}, bf16[1,32,2560]{2,1,0:T(8,128)(2,1)S(1)}, u32[]{:S(2)}, u32[]{:S(2)}) %collective-permute-start) | collective-permute-done | bytes 163872 | tf_op jit(solution)/shard_map/while/body/eval_jaxpr/ppermute | solution.py:16
  115.0 12.6 %conditional.2 = (bf16[1,32,2560]{2,1,0:T(8,128)(2,1)S(1)}, f32[1,1,40,64,128]{4,3,2,1,0:T(8,128)S(1)}, bf16[1,1,128,2560]{3,2,1,0:T(8,128)(2,1)}, bf16[1,1,128,256]{3,2,1,0:T(8,128)(2,1)}) conditional(s32[]{:T(128)} %convert_element_type.236, (f32[1,1,40,64,128]{4,3,2,1,0:T(8,128)S(1)}, bf16[1,1,128,2560]{3,2,1,0:T(8,128)(2,1)}, ...), branch_computations={%region_4.4_spmd, %region_5.7_spmd} | conditional | flops 140346368 | bytes 16897460 | solution.py:159
  120.4 1.4 fusion.13
  124.4 2.5 %bitcast_dynamic-update-slice_fusion = (bf16[1,1,128,2560]{3,2,1,0:T(8,128)(2,1)}, bf16[1,32,2560]{2,1,0:T(8,128)(2,1)S(1)}) fusion(bf16[1,1,128,2560]{3,2,1,0:T(8,128)(2,1)} %get-tuple-element.483, s32[]{:T(128)S(6)} %select_n.90, bf16[1,2560,256]{2,1,0:T(8,128)(2,1)} %get-tuple-element.482, bf16[32,128]{1,0:T(8,128)(2,1)S(1)} %fusion.13, ...), kind=kOutput, calls=%fused_computation.46 | convolution fusion | flops 42303488 | bytes 2146308 | tf_op jit(solution)/shard_map/while/body/eval_jaxpr/cond/branch_1_fun/vmap()/dot_general | solution.py:84
  128.9 5.9 %collective-permute-done = bf16[1,32,2560]{2,1,0:T(8,128)(2,1)S(1)} collective-permute-done((bf16[1,32,2560]{2,1,0:T(8,128)(2,1)S(1)}, bf16[1,32,2560]{2,1,0:T(8,128)(2,1)S(1)}, u32[]{:S(2)}, u32[]{:S(2)}) %collective-permute-start) | collective-permute-done | bytes 163872 | tf_op jit(solution)/shard_map/while/body/eval_jaxpr/ppermute | solution.py:16
  134.8 12.6 %conditional.2 = (bf16[1,32,2560]{2,1,0:T(8,128)(2,1)S(1)}, f32[1,1,40,64,128]{4,3,2,1,0:T(8,128)S(1)}, bf16[1,1,128,2560]{3,2,1,0:T(8,128)(2,1)}, bf16[1,1,128,256]{3,2,1,0:T(8,128)(2,1)}) conditional(s32[]{:T(128)} %convert_element_type.236, (f32[1,1,40,64,128]{4,3,2,1,0:T(8,128)S(1)}, bf16[1,1,128,2560]{3,2,1,0:T(8,128)(2,1)}, ...), branch_computations={%region_4.4_spmd, %region_5.7_spmd} | conditional | flops 140346368 | bytes 16897460 | solution.py:159
  144.2 2.5 %bitcast_dynamic-update-slice_fusion = (bf16[1,1,128,2560]{3,2,1,0:T(8,128)(2,1)}, bf16[1,32,2560]{2,1,0:T(8,128)(2,1)S(1)}) fusion(bf16[1,1,128,2560]{3,2,1,0:T(8,128)(2,1)} %get-tuple-element.483, s32[]{:T(128)S(6)} %select_n.90, bf16[1,2560,256]{2,1,0:T(8,128)(2,1)} %get-tuple-element.482, bf16[32,128]{1,0:T(8,128)(2,1)S(1)} %fusion.13, ...), kind=kOutput, calls=%fused_computation.46 | convolution fusion | flops 42303488 | bytes 2146308 | tf_op jit(solution)/shard_map/while/body/eval_jaxpr/cond/branch_1_fun/vmap()/dot_general | solution.py:84
  148.7 5.9 %collective-permute-done = bf16[1,32,2560]{2,1,0:T(8,128)(2,1)S(1)} collective-permute-done((bf16[1,32,2560]{2,1,0:T(8,128)(2,1)S(1)}, bf16[1,32,2560]{2,1,0:T(8,128)(2,1)S(1)}, u32[]{:S(2)}, u32[]{:S(2)}) %collective-permute-start) | collective-permute-done | bytes 163872 | tf_op jit(solution)/shard_map/while/body/eval_jaxpr/ppermute | solution.py:16
  154.6 12.6 %conditional.2 = (bf16[1,32,2560]{2,1,0:T(8,128)(2,1)S(1)}, f32[1,1,40,64,128]{4,3,2,1,0:T(8,128)S(1)}, bf16[1,1,128,2560]{3,2,1,0:T(8,128)(2,1)}, bf16[1,1,128,256]{3,2,1,0:T(8,128)(2,1)}) conditional(s32[]{:T(128)} %convert_element_type.236, (f32[1,1,40,64,128]{4,3,2,1,0:T(8,128)S(1)}, bf16[1,1,128,2560]{3,2,1,0:T(8,128)(2,1)}, ...), branch_computations={%region_4.4_spmd, %region_5.7_spmd} | conditional | flops 140346368 | bytes 16897460 | solution.py:159
  164.0 2.5 %bitcast_dynamic-update-slice_fusion = (bf16[1,1,128,2560]{3,2,1,0:T(8,128)(2,1)}, bf16[1,32,2560]{2,1,0:T(8,128)(2,1)S(1)}) fusion(bf16[1,1,128,2560]{3,2,1,0:T(8,128)(2,1)} %get-tuple-element.483, s32[]{:T(128)S(6)} %select_n.90, bf16[1,2560,256]{2,1,0:T(8,128)(2,1)} %get-tuple-element.482, bf16[32,128]{1,0:T(8,128)(2,1)S(1)} %fusion.13, ...), kind=kOutput, calls=%fused_computation.46 | convolution fusion | flops 42303488 | bytes 2146308 | tf_op jit(solution)/shard_map/while/body/eval_jaxpr/cond/branch_1_fun/vmap()/dot_general | solution.py:84
  168.5 5.9 %collective-permute-done = bf16[1,32,2560]{2,1,0:T(8,128)(2,1)S(1)} collective-permute-done((bf16[1,32,2560]{2,1,0:T(8,128)(2,1)S(1)}, bf16[1,32,2560]{2,1,0:T(8,128)(2,1)S(1)}, u32[]{:S(2)}, u32[]{:S(2)}) %collective-permute-start) | collective-permute-done | bytes 163872 | tf_op jit(solution)/shard_map/while/body/eval_jaxpr/ppermute | solution.py:16
  174.4 10.2 %all-gather = bf16[1,1,1024,256]{3,2,1,0:T(8,128)(2,1)S(1)} all-gather(bf16[1,1,128,256]{3,2,1,0:T(8,128)(2,1)} %get-tuple-element.508), channel_id=2, replica_groups=mesh['section'=4,'dp'=8] {'dp'}, dimensions={2}, use_global_device_ids=true | all-gather | bytes 589824 | tf_op jit(solution)/shard_map/all_gather | solution.py:181
  184.6 2.3 %reshape.677 = bf16[2560,1,128]{2,1,0:T(2,128)(2,1)S(1)} reshape(bf16[8,2,20480]{2,1,0:T(2,128)(2,1)} %all-to-all-done) | data formatting | bytes 1310720
  (185 shorter events, 58.0 us)
Async XLA Ops:
  17.9 6.2 %copy-start.1 = (f32[1,1,128,40]{2,3,1,0:T(8,128)S(1)}, f32[1,1,128,40]{2,3,1,0:T(8,128)}, u32[]{:S(2)}) copy-start(f32[1,1,128,40]{2,3,1,0:T(8,128)} %param.16) | copy-start | bytes 61444
  18.9 165.6 %all-to-all-start = ((bf16[8,2,20480]{2,1,0:T(2,128)(2,1)}), bf16[8,2,20480]{2,1,0:T(2,128)(2,1)}, u32[]{:S(2)}, u32[]{:S(2)}) async-start(bf16[8,2,20480]{2,1,0:T(2,128)(2,1)} %reshape.676), calls=%async_computation | async-start | bytes 1310720 | tf_op jit(solution)/shard_map/all_to_all | solution.py:179
  26.7 1.6 copy-start
  35.0 8.7 %collective-permute-start = (bf16[1,32,2560]{2,1,0:T(8,128)(2,1)S(1)}, bf16[1,32,2560]{2,1,0:T(8,128)(2,1)S(1)}, u32[]{:S(2)}, u32[]{:S(2)}) collective-permute-start(bf16[1,32,2560]{2,1,0:T(8,128)(2,1)S(1)} %get-tuple-element.684), channel_id=1, source_target_pairs={{8,0},{16,8},{24,16},{9,1},{17,9},{25,17},{10,2},{18,10},{26,18},{... | collective-permute-start | bytes 491528 | tf_op jit(solution)/shard_map/while/body/eval_jaxpr/ppermute | solution.py:16
  43.7 7.7 %collective-permute-start = (bf16[1,32,2560]{2,1,0:T(8,128)(2,1)S(1)}, bf16[1,32,2560]{2,1,0:T(8,128)(2,1)S(1)}, u32[]{:S(2)}, u32[]{:S(2)}) collective-permute-start(bf16[1,32,2560]{2,1,0:T(8,128)(2,1)S(1)} %get-tuple-element.684), channel_id=1, source_target_pairs={{8,0},{16,8},{24,16},{9,1},{17,9},{25,17},{10,2},{18,10},{26,18},{... | collective-permute-start | bytes 491528 | tf_op jit(solution)/shard_map/while/body/eval_jaxpr/ppermute | solution.py:16
  51.4 43.8 %collective-permute-start = (bf16[1,32,2560]{2,1,0:T(8,128)(2,1)S(1)}, bf16[1,32,2560]{2,1,0:T(8,128)(2,1)S(1)}, u32[]{:S(2)}, u32[]{:S(2)}) collective-permute-start(bf16[1,32,2560]{2,1,0:T(8,128)(2,1)S(1)} %get-tuple-element.684), channel_id=1, source_target_pairs={{8,0},{16,8},{24,16},{9,1},{17,9},{25,17},{10,2},{18,10},{26,18},{... | collective-permute-start | bytes 491528 | tf_op jit(solution)/shard_map/while/body/eval_jaxpr/ppermute | solution.py:16
  107.8 7.2 %collective-permute-start = (bf16[1,32,2560]{2,1,0:T(8,128)(2,1)S(1)}, bf16[1,32,2560]{2,1,0:T(8,128)(2,1)S(1)}, u32[]{:S(2)}, u32[]{:S(2)}) collective-permute-start(bf16[1,32,2560]{2,1,0:T(8,128)(2,1)S(1)} %get-tuple-element.684), channel_id=1, source_target_pairs={{8,0},{16,8},{24,16},{9,1},{17,9},{25,17},{10,2},{18,10},{26,18},{... | collective-permute-start | bytes 491528 | tf_op jit(solution)/shard_map/while/body/eval_jaxpr/ppermute | solution.py:16
  127.6 7.2 %collective-permute-start = (bf16[1,32,2560]{2,1,0:T(8,128)(2,1)S(1)}, bf16[1,32,2560]{2,1,0:T(8,128)(2,1)S(1)}, u32[]{:S(2)}, u32[]{:S(2)}) collective-permute-start(bf16[1,32,2560]{2,1,0:T(8,128)(2,1)S(1)} %get-tuple-element.684), channel_id=1, source_target_pairs={{8,0},{16,8},{24,16},{9,1},{17,9},{25,17},{10,2},{18,10},{26,18},{... | collective-permute-start | bytes 491528 | tf_op jit(solution)/shard_map/while/body/eval_jaxpr/ppermute | solution.py:16
  147.4 7.2 %collective-permute-start = (bf16[1,32,2560]{2,1,0:T(8,128)(2,1)S(1)}, bf16[1,32,2560]{2,1,0:T(8,128)(2,1)S(1)}, u32[]{:S(2)}, u32[]{:S(2)}) collective-permute-start(bf16[1,32,2560]{2,1,0:T(8,128)(2,1)S(1)} %get-tuple-element.684), channel_id=1, source_target_pairs={{8,0},{16,8},{24,16},{9,1},{17,9},{25,17},{10,2},{18,10},{26,18},{... | collective-permute-start | bytes 491528 | tf_op jit(solution)/shard_map/while/body/eval_jaxpr/ppermute | solution.py:16
  167.2 7.2 %collective-permute-start = (bf16[1,32,2560]{2,1,0:T(8,128)(2,1)S(1)}, bf16[1,32,2560]{2,1,0:T(8,128)(2,1)S(1)}, u32[]{:S(2)}, u32[]{:S(2)}) collective-permute-start(bf16[1,32,2560]{2,1,0:T(8,128)(2,1)S(1)} %get-tuple-element.684), channel_id=1, source_target_pairs={{8,0},{16,8},{24,16},{9,1},{17,9},{25,17},{10,2},{18,10},{26,18},{... | collective-permute-start | bytes 491528 | tf_op jit(solution)/shard_map/while/body/eval_jaxpr/ppermute | solution.py:16
where the time goes:
time: 190 us; the launch traced here: 189 us
  waiting for transfers between devices  79.9 us (42%)
  matrix products  30.2 us (16%)
  other arithmetic  28.2 us (15%)
  local copies, waits for them, and re-layouts  24.2 us (13%)
  starting transfers between devices  14.2 us (7%)
  blocking collectives  10.2 us (5%)
    ppermute x7, waiting for transfers between devices, passed_along(): return lax.ppermute(block, axis, route)  79.9 us
    unnamed x1, other arithmetic  14.3 us
    all_gather x1, blocking collectives, shards(): maps_all = lax.all_gather(maps_here, 'dp', axis=1, tiled=True)  10.2 us
    dot_general x4, matrix products, block_back(): lax.dot_general(grad_bc, weights, (((1,), (1,)), ((), ())), preferred_ele...  9.94 us
    ppermute x7, starting transfers between devices, passed_along(): return lax.ppermute(block, axis, route)  9.04 us
    dot_general x4, matrix products, block_terms(): jnp.einsum('ihp,hpn->in', lead_grads, state_b, preferred_element_type=jnp...  5.47 us
    all_to_all x1, starting transfers between devices, shards(): rows_all = lax.all_to_all(rows_here, 'dp', 2, 1, tiled=True)  5.17 us
    unnamed x8, local copies, waits for them, and re-layouts  4 us
  transfers between devices with their start and end apart: 8, of which 7 were waited for; matrix products, arithmetic and copies ran while one was open for 32% of the time, Pallas kernels for 0%

commit v1 on v0

--- a/solution.py
+++ b/solution.py
@@ -178,7 +178,12 @@
     rows_here = layer_inputs.reshape(lay_dev, seq_dev * tok_len, features)
     rows_all = lax.all_to_all(rows_here, "dp", 2, 1, tiled=True)
     maps_here = map_store.reshape(lay_dev, seq_dev * tok_len, map_store.shape[-1])
-    maps_all = lax.all_gather(maps_here, "dp", axis=1, tiled=True)
+    ring = [maps_here]
+    for hop in range(7):
+        ring.append(lax.ppermute(ring[-1], "dp", [(dev, (dev + 1) % 8) for dev in range(8)]))
+    maps_all = jnp.roll(
+        jnp.concatenate(ring[::-1], axis=1), (lax.axis_index("dp") + 1) * ring[0].shape[1], axis=1
+    )
     grad_w = (
         jnp.einsum("lrd,lrc->ldc", rows_all, maps_all, preferred_element_type=jnp.float32) / divisor
     )

time: 190 us -> 218 us (1.15)
  waiting for transfers between devices: 79.9 us -> 109 us
  local copies, waits for them, and re-layouts: 24.2 us -> 36.4 us
  blocking collectives: 10.2 us -> 0 us
  other arithmetic: 28.2 us -> 25.7 us
    ppermute x0 -> x7, waiting for transfers between devices: none -> 27.5 us  [shards(): lax.ppermute(ring[-1], 'dp', [(dev, (dev + 1) % 8) for dev in range(8)])]
    all_gather x1 -> x0, blocking collectives: 10.2 us -> none  [shards(): maps_all = lax.all_gather(maps_here, 'dp', axis=1, tiled=True)]
    unnamed x8 -> x23, local copies, waits for them, and re-layouts: 4 us -> 11.8 us
    dynamic_slice x4, local copies, waits for them, and re-layouts: 0.04 us -> 2.91 us  [compute(): lax.dynamic_slice_in_dim(bc_all[level_no], row_start, block_len, 1)]
    scatter x4, other arithmetic: 2.46 us -> 0.04 us  [compute(): maps_in.at[level_no]]
  transfers between devices with their start and end apart: 8 -> 15, of which waited for: 7 -> 14; matrix products, arithmetic and copies ran while one was open for 32% -> 13% of each run, Pallas kernels for 0% -> 0%
where the time goes in v1:
time: 218 us; the launch traced here: 217 us
  waiting for transfers between devices  109 us (50%)
  local copies, waits for them, and re-layouts  36.4 us (17%)
  matrix products  31.3 us (14%)
  other arithmetic  25.7 us (12%)
  starting transfers between devices  13 us (6%)
    ppermute x7, waiting for transfers between devices, passed_along(): return lax.ppermute(block, axis, route)  80.1 us
    ppermute x7, waiting for transfers between devices, shards(): lax.ppermute(ring[-1], 'dp', [(dev, (dev + 1) % 8) for dev in range(8)])  27.5 us
    unnamed x1, other arithmetic  14.3 us
    unnamed x23, local copies, waits for them, and re-layouts  11.8 us
    dot_general x4, matrix products, block_back(): lax.dot_general(grad_bc, weights, (((1,), (1,)), ((), ())), preferred_ele...  9.95 us
    ppermute x7, starting transfers between devices, passed_along(): return lax.ppermute(block, axis, route)  9.04 us
    dot_general x4, matrix products, block_terms(): jnp.einsum('ihp,hpn->in', lead_grads, state_b, preferred_element_type=jnp...  5.46 us
  transfers between devices with their start and end apart: 15, of which 14 were waited for; matrix products, arithmetic and copies ran while one was open for 13% of the time, Pallas kernels for 0%

profile of v1, /device:TPU:0, one launch (start us, length us, event | category | flops | bytes accessed | tf_op | source)
XLA Modules:
  0.0 216.9 jit_solution(15368246612912595782)
XLA Ops:
  12.4 140.2 %while.24 = (s32[]{:T(128)}, bf16[1,32,2560]{2,1,0:T(8,128)(2,1)S(1)}, f32[1,1,40,64,128]{4,3,2,1,0:T(8,128)S(1)}, bf16[1,1,128,2560]{3,2,1,0:T(8,128)(2,1)}, bf...) while((s32[]{:T(128)}, ...), condition=%wide.region_8.9_spmd, body=%wide.region_3.8_spmd.sunk | while | flops 140346368 | bytes 17553168 | solution.py:173
  13.8 7.8 %collective-permute-done = bf16[1,32,2560]{2,1,0:T(8,128)(2,1)S(1)} collective-permute-done((bf16[1,32,2560]{2,1,0:T(8,128)(2,1)S(1)}, bf16[1,32,2560]{2,1,0:T(8,128)(2,1)S(1)}, u32[]{:S(2)}, u32[]{:S(2)}) %collective-permute-start) | collective-permute-done | bytes 163872 | tf_op jit(solution)/shard_map/while/body/eval_jaxpr/ppermute | solution.py:16
  23.0 6.0 %collective-permute-done = bf16[1,32,2560]{2,1,0:T(8,128)(2,1)S(1)} collective-permute-done((bf16[1,32,2560]{2,1,0:T(8,128)(2,1)S(1)}, bf16[1,32,2560]{2,1,0:T(8,128)(2,1)S(1)}, u32[]{:S(2)}, u32[]{:S(2)}) %collective-permute-start) | collective-permute-done | bytes 163872 | tf_op jit(solution)/shard_map/while/body/eval_jaxpr/ppermute | solution.py:16
  30.3 42.7 %collective-permute-done = bf16[1,32,2560]{2,1,0:T(8,128)(2,1)S(1)} collective-permute-done((bf16[1,32,2560]{2,1,0:T(8,128)(2,1)S(1)}, bf16[1,32,2560]{2,1,0:T(8,128)(2,1)S(1)}, u32[]{:S(2)}, u32[]{:S(2)}) %collective-permute-start) | collective-permute-done | bytes 163872 | tf_op jit(solution)/shard_map/while/body/eval_jaxpr/ppermute | solution.py:16
  73.0 12.7 %conditional.2 = (bf16[1,32,2560]{2,1,0:T(8,128)(2,1)S(1)}, f32[1,1,40,64,128]{4,3,2,1,0:T(8,128)S(1)}, bf16[1,1,128,2560]{3,2,1,0:T(8,128)(2,1)}, bf16[1,1,128,256]{3,2,1,0:T(8,128)(2,1)S(1)}) conditional(s32[]{:T(128)} %convert_element_type.236, (f32[1,1,40,64,128]{4,3,2,1,0:T(8,128)S(1)}, bf16[1,1,128,2560]{3,2,1,0:T(8,128)(2,1)}, ...), branch_computations={%region_4.4_spmd, %region_5.7_spmd} | conditional | flops 140346368 | bytes 16897460 | solution.py:159
  82.4 2.5 %bitcast_dynamic-update-slice_fusion = (bf16[1,1,128,2560]{3,2,1,0:T(8,128)(2,1)}, bf16[1,32,2560]{2,1,0:T(8,128)(2,1)S(1)}) fusion(bf16[1,1,128,2560]{3,2,1,0:T(8,128)(2,1)} %get-tuple-element.483, s32[]{:T(128)S(6)} %select_n.101, bf16[1,2560,256]{2,1,0:T(8,128)(2,1)} %get-tuple-element.482, bf16[32,128]{1,0:T(8,128)(2,1)S(1)} %fusion.13, ...), kind=kOutput, calls=%fused_computation.46 | convolution fusion | flops 42303488 | bytes 2146308 | tf_op jit(solution)/shard_map/while/body/eval_jaxpr/cond/branch_1_fun/vmap()/dot_general | solution.py:84
  87.0 5.9 %collective-permute-done = bf16[1,32,2560]{2,1,0:T(8,128)(2,1)S(1)} collective-permute-done((bf16[1,32,2560]{2,1,0:T(8,128)(2,1)S(1)}, bf16[1,32,2560]{2,1,0:T(8,128)(2,1)S(1)}, u32[]{:S(2)}, u32[]{:S(2)}) %collective-permute-start) | collective-permute-done | bytes 163872 | tf_op jit(solution)/shard_map/while/body/eval_jaxpr/ppermute | solution.py:16
  92.9 12.7 %conditional.2 = (bf16[1,32,2560]{2,1,0:T(8,128)(2,1)S(1)}, f32[1,1,40,64,128]{4,3,2,1,0:T(8,128)S(1)}, bf16[1,1,128,2560]{3,2,1,0:T(8,128)(2,1)}, bf16[1,1,128,256]{3,2,1,0:T(8,128)(2,1)S(1)}) conditional(s32[]{:T(128)} %convert_element_type.236, (f32[1,1,40,64,128]{4,3,2,1,0:T(8,128)S(1)}, bf16[1,1,128,2560]{3,2,1,0:T(8,128)(2,1)}, ...), branch_computations={%region_4.4_spmd, %region_5.7_spmd} | conditional | flops 140346368 | bytes 16897460 | solution.py:159
  102.4 2.5 %bitcast_dynamic-update-slice_fusion = (bf16[1,1,128,2560]{3,2,1,0:T(8,128)(2,1)}, bf16[1,32,2560]{2,1,0:T(8,128)(2,1)S(1)}) fusion(bf16[1,1,128,2560]{3,2,1,0:T(8,128)(2,1)} %get-tuple-element.483, s32[]{:T(128)S(6)} %select_n.101, bf16[1,2560,256]{2,1,0:T(8,128)(2,1)} %get-tuple-element.482, bf16[32,128]{1,0:T(8,128)(2,1)S(1)} %fusion.13, ...), kind=kOutput, calls=%fused_computation.46 | convolution fusion | flops 42303488 | bytes 2146308 | tf_op jit(solution)/shard_map/while/body/eval_jaxpr/cond/branch_1_fun/vmap()/dot_general | solution.py:84
  106.9 5.9 %collective-permute-done = bf16[1,32,2560]{2,1,0:T(8,128)(2,1)S(1)} collective-permute-done((bf16[1,32,2560]{2,1,0:T(8,128)(2,1)S(1)}, bf16[1,32,2560]{2,1,0:T(8,128)(2,1)S(1)}, u32[]{:S(2)}, u32[]{:S(2)}) %collective-permute-start) | collective-permute-done | bytes 163872 | tf_op jit(solution)/shard_map/while/body/eval_jaxpr/ppermute | solution.py:16
  112.8 12.7 %conditional.2 = (bf16[1,32,2560]{2,1,0:T(8,128)(2,1)S(1)}, f32[1,1,40,64,128]{4,3,2,1,0:T(8,128)S(1)}, bf16[1,1,128,2560]{3,2,1,0:T(8,128)(2,1)}, bf16[1,1,128,256]{3,2,1,0:T(8,128)(2,1)S(1)}) conditional(s32[]{:T(128)} %convert_element_type.236, (f32[1,1,40,64,128]{4,3,2,1,0:T(8,128)S(1)}, bf16[1,1,128,2560]{3,2,1,0:T(8,128)(2,1)}, ...), branch_computations={%region_4.4_spmd, %region_5.7_spmd} | conditional | flops 140346368 | bytes 16897460 | solution.py:159
  122.3 2.5 %bitcast_dynamic-update-slice_fusion = (bf16[1,1,128,2560]{3,2,1,0:T(8,128)(2,1)}, bf16[1,32,2560]{2,1,0:T(8,128)(2,1)S(1)}) fusion(bf16[1,1,128,2560]{3,2,1,0:T(8,128)(2,1)} %get-tuple-element.483, s32[]{:T(128)S(6)} %select_n.101, bf16[1,2560,256]{2,1,0:T(8,128)(2,1)} %get-tuple-element.482, bf16[32,128]{1,0:T(8,128)(2,1)S(1)} %fusion.13, ...), kind=kOutput, calls=%fused_computation.46 | convolution fusion | flops 42303488 | bytes 2146308 | tf_op jit(solution)/shard_map/while/body/eval_jaxpr/cond/branch_1_fun/vmap()/dot_general | solution.py:84
  126.8 5.9 %collective-permute-done = bf16[1,32,2560]{2,1,0:T(8,128)(2,1)S(1)} collective-permute-done((bf16[1,32,2560]{2,1,0:T(8,128)(2,1)S(1)}, bf16[1,32,2560]{2,1,0:T(8,128)(2,1)S(1)}, u32[]{:S(2)}, u32[]{:S(2)}) %collective-permute-start) | collective-permute-done | bytes 163872 | tf_op jit(solution)/shard_map/while/body/eval_jaxpr/ppermute | solution.py:16
  132.7 12.7 %conditional.2 = (bf16[1,32,2560]{2,1,0:T(8,128)(2,1)S(1)}, f32[1,1,40,64,128]{4,3,2,1,0:T(8,128)S(1)}, bf16[1,1,128,2560]{3,2,1,0:T(8,128)(2,1)}, bf16[1,1,128,256]{3,2,1,0:T(8,128)(2,1)S(1)}) conditional(s32[]{:T(128)} %convert_element_type.236, (f32[1,1,40,64,128]{4,3,2,1,0:T(8,128)S(1)}, bf16[1,1,128,2560]{3,2,1,0:T(8,128)(2,1)}, ...), branch_computations={%region_4.4_spmd, %region_5.7_spmd} | conditional | flops 140346368 | bytes 16897460 | solution.py:159
  146.7 5.9 %collective-permute-done = bf16[1,32,2560]{2,1,0:T(8,128)(2,1)S(1)} collective-permute-done((bf16[1,32,2560]{2,1,0:T(8,128)(2,1)S(1)}, bf16[1,32,2560]{2,1,0:T(8,128)(2,1)S(1)}, u32[]{:S(2)}, u32[]{:S(2)}) %collective-permute-start) | collective-permute-done | bytes 163872 | tf_op jit(solution)/shard_map/while/body/eval_jaxpr/ppermute | solution.py:16
  152.6 4.6 %collective-permute-done.1 = bf16[1,128,256]{2,1,0:T(8,128)(2,1)S(1)} collective-permute-done((bf16[1,128,256]{2,1,0:T(8,128)(2,1)S(1)}, bf16[1,128,256]{2,1,0:T(8,128)(2,1)S(1)}, u32[]{:S(2)}, u32[]{:S(2)}) %collective-permute-start.1) | collective-permute-done | bytes 65568 | tf_op jit(solution)/shard_map/ppermute | solution.py:183
  157.2 4.6 %collective-permute-done.2 = bf16[1,128,256]{2,1,0:T(8,128)(2,1)S(1)} collective-permute-done((bf16[1,128,256]{2,1,0:T(8,128)(2,1)S(1)}, bf16[1,128,256]{2,1,0:T(8,128)(2,1)S(1)}, u32[]{:S(2)}, u32[]{:S(2)}) %collective-permute-start.2) | collective-permute-done | bytes 65568 | tf_op jit(solution)/shard_map/ppermute | solution.py:183
  161.8 4.6 %collective-permute-done.3 = bf16[1,128,256]{2,1,0:T(8,128)(2,1)S(1)} collective-permute-done((bf16[1,128,256]{2,1,0:T(8,128)(2,1)S(1)}, bf16[1,128,256]{2,1,0:T(8,128)(2,1)S(1)}, u32[]{:S(2)}, u32[]{:S(2)}) %collective-permute-start.3) | collective-permute-done | bytes 65568 | tf_op jit(solution)/shard_map/ppermute | solution.py:183
  166.4 4.6 %collective-permute-done.4 = bf16[1,128,256]{2,1,0:T(8,128)(2,1)S(1)} collective-permute-done((bf16[1,128,256]{2,1,0:T(8,128)(2,1)S(1)}, bf16[1,128,256]{2,1,0:T(8,128)(2,1)S(1)}, u32[]{:S(2)}, u32[]{:S(2)}) %collective-permute-start.4) | collective-permute-done | bytes 65568 | tf_op jit(solution)/shard_map/ppermute | solution.py:183
  170.9 4.6 %collective-permute-done.5 = bf16[1,128,256]{2,1,0:T(8,128)(2,1)S(1)} collective-permute-done((bf16[1,128,256]{2,1,0:T(8,128)(2,1)S(1)}, bf16[1,128,256]{2,1,0:T(8,128)(2,1)S(1)}, u32[]{:S(2)}, u32[]{:S(2)}) %collective-permute-start.5) | collective-permute-done | bytes 65568 | tf_op jit(solution)/shard_map/ppermute | solution.py:183
  175.5 4.6 %collective-permute-done.6 = bf16[1,128,256]{2,1,0:T(8,128)(2,1)S(1)} collective-permute-done((bf16[1,128,256]{2,1,0:T(8,128)(2,1)S(1)}, bf16[1,128,256]{2,1,0:T(8,128)(2,1)S(1)}, u32[]{:S(2)}, u32[]{:S(2)}) %collective-permute-start.6) | collective-permute-done | bytes 65568 | tf_op jit(solution)/shard_map/ppermute | solution.py:183
  180.1 2.5 %copy.89 = bf16[1,128,2560]{1,0,2:T(2,128)(2,1)S(1)} copy(bf16[1,128,2560]{2,1,0:T(8,128)(2,1)} %bitcast.44) | data formatting | bytes 1310720 | tf_op jit(solution)/shard_map/reshape | solution.py:178
  183.2 14.3 %reduce.10 = bf16[2560,128]{1,0:T(8,128)(2,1)S(1)} reduce(bf16[2560,1,128]{2,1,0:T(2,128)(2,1)S(1)} %bitcast.181, bf16[]{:T(256)} %broadcast.354), dimensions={1}, to_apply=%bitcast.173.reduce_sub_computation | reduce | bytes 1310722
  198.4 4.0 %all-to-all-start = ((bf16[8,2,20480]{2,1,0:T(2,128)(2,1)}), bf16[8,2,20480]{2,1,0:T(2,128)(2,1)S(1)}, u32[]{:S(2)}, u32[]{:S(2)}) async-start(bf16[8,2,20480]{2,1,0:T(2,128)(2,1)} %reshape.674), calls=%async_computation | async-start | bytes 1310720 | tf_op jit(solution)/shard_map/all_to_all | solution.py:179
  (214 shorter events, 79.5 us)
Async XLA Ops:
  4.8 1.6 copy-start
  7.8 1.2 copy-start.1
  12.5 9.1 %collective-permute-start = (bf16[1,32,2560]{2,1,0:T(8,128)(2,1)S(1)}, bf16[1,32,2560]{2,1,0:T(8,128)(2,1)S(1)}, u32[]{:S(2)}, u32[]{:S(2)}) collective-permute-start(bf16[1,32,2560]{2,1,0:T(8,128)(2,1)S(1)} %get-tuple-element.684), channel_id=1, source_target_pairs={{8,0},{16,8},{24,16},{9,1},{17,9},{25,17},{10,2},{18,10},{26,18},{... | collective-permute-start | bytes 491528 | tf_op jit(solution)/shard_map/while/body/eval_jaxpr/ppermute | solution.py:16
  21.7 7.3 %collective-permute-start = (bf16[1,32,2560]{2,1,0:T(8,128)(2,1)S(1)}, bf16[1,32,2560]{2,1,0:T(8,128)(2,1)S(1)}, u32[]{:S(2)}, u32[]{:S(2)}) collective-permute-start(bf16[1,32,2560]{2,1,0:T(8,128)(2,1)S(1)} %get-tuple-element.684), channel_id=1, source_target_pairs={{8,0},{16,8},{24,16},{9,1},{17,9},{25,17},{10,2},{18,10},{26,18},{... | collective-permute-start | bytes 491528 | tf_op jit(solution)/shard_map/while/body/eval_jaxpr/ppermute | solution.py:16
  29.0 44.0 %collective-permute-start = (bf16[1,32,2560]{2,1,0:T(8,128)(2,1)S(1)}, bf16[1,32,2560]{2,1,0:T(8,128)(2,1)S(1)}, u32[]{:S(2)}, u32[]{:S(2)}) collective-permute-start(bf16[1,32,2560]{2,1,0:T(8,128)(2,1)S(1)} %get-tuple-element.684), channel_id=1, source_target_pairs={{8,0},{16,8},{24,16},{9,1},{17,9},{25,17},{10,2},{18,10},{26,18},{... | collective-permute-start | bytes 491528 | tf_op jit(solution)/shard_map/while/body/eval_jaxpr/ppermute | solution.py:16
  85.6 7.2 %collective-permute-start = (bf16[1,32,2560]{2,1,0:T(8,128)(2,1)S(1)}, bf16[1,32,2560]{2,1,0:T(8,128)(2,1)S(1)}, u32[]{:S(2)}, u32[]{:S(2)}) collective-permute-start(bf16[1,32,2560]{2,1,0:T(8,128)(2,1)S(1)} %get-tuple-element.684), channel_id=1, source_target_pairs={{8,0},{16,8},{24,16},{9,1},{17,9},{25,17},{10,2},{18,10},{26,18},{... | collective-permute-start | bytes 491528 | tf_op jit(solution)/shard_map/while/body/eval_jaxpr/ppermute | solution.py:16
  105.6 7.2 %collective-permute-start = (bf16[1,32,2560]{2,1,0:T(8,128)(2,1)S(1)}, bf16[1,32,2560]{2,1,0:T(8,128)(2,1)S(1)}, u32[]{:S(2)}, u32[]{:S(2)}) collective-permute-start(bf16[1,32,2560]{2,1,0:T(8,128)(2,1)S(1)} %get-tuple-element.684), channel_id=1, source_target_pairs={{8,0},{16,8},{24,16},{9,1},{17,9},{25,17},{10,2},{18,10},{26,18},{... | collective-permute-start | bytes 491528 | tf_op jit(solution)/shard_map/while/body/eval_jaxpr/ppermute | solution.py:16
  125.5 7.2 %collective-permute-start = (bf16[1,32,2560]{2,1,0:T(8,128)(2,1)S(1)}, bf16[1,32,2560]{2,1,0:T(8,128)(2,1)S(1)}, u32[]{:S(2)}, u32[]{:S(2)}) collective-permute-start(bf16[1,32,2560]{2,1,0:T(8,128)(2,1)S(1)} %get-tuple-element.684), channel_id=1, source_target_pairs={{8,0},{16,8},{24,16},{9,1},{17,9},{25,17},{10,2},{18,10},{26,18},{... | collective-permute-start | bytes 491528 | tf_op jit(solution)/shard_map/while/body/eval_jaxpr/ppermute | solution.py:16
  145.4 7.2 %collective-permute-start = (bf16[1,32,2560]{2,1,0:T(8,128)(2,1)S(1)}, bf16[1,32,2560]{2,1,0:T(8,128)(2,1)S(1)}, u32[]{:S(2)}, u32[]{:S(2)}) collective-permute-start(bf16[1,32,2560]{2,1,0:T(8,128)(2,1)S(1)} %get-tuple-element.684), channel_id=1, source_target_pairs={{8,0},{16,8},{24,16},{9,1},{17,9},{25,17},{10,2},{18,10},{26,18},{... | collective-permute-start | bytes 491528 | tf_op jit(solution)/shard_map/while/body/eval_jaxpr/ppermute | solution.py:16
  152.6 4.6 %collective-permute-start.1 = (bf16[1,128,256]{2,1,0:T(8,128)(2,1)S(1)}, bf16[1,128,256]{2,1,0:T(8,128)(2,1)S(1)}, u32[]{:S(2)}, u32[]{:S(2)}) collective-permute-start(bf16[1,128,256]{2,1,0:T(8,128)(2,1)S(1)} %bitcast.188), channel_id=1, source_target_pairs={{0,1},{1,2},{2,3},{3,4},{4,5},{5,6},{6,7},{7,0},{8,9},{9,10},{10,1... | collective-permute-start | bytes 196616 | tf_op jit(solution)/shard_map/ppermute | solution.py:183
  157.2 4.6 %collective-permute-start.2 = (bf16[1,128,256]{2,1,0:T(8,128)(2,1)S(1)}, bf16[1,128,256]{2,1,0:T(8,128)(2,1)S(1)}, u32[]{:S(2)}, u32[]{:S(2)}) collective-permute-start(bf16[1,128,256]{2,1,0:T(8,128)(2,1)S(1)} %collective-permute-done.1), channel_id=1, source_target_pairs={{0,1},{1,2},{2,3},{3,4},{4,5},{5,6},{6,7},{7,0},{8,9},{9,10},{10,1... | collective-permute-start | bytes 196616 | tf_op jit(solution)/shard_map/ppermute | solution.py:183
  161.8 4.6 %collective-permute-start.3 = (bf16[1,128,256]{2,1,0:T(8,128)(2,1)S(1)}, bf16[1,128,256]{2,1,0:T(8,128)(2,1)S(1)}, u32[]{:S(2)}, u32[]{:S(2)}) collective-permute-start(bf16[1,128,256]{2,1,0:T(8,128)(2,1)S(1)} %collective-permute-done.2), channel_id=1, source_target_pairs={{0,1},{1,2},{2,3},{3,4},{4,5},{5,6},{6,7},{7,0},{8,9},{9,10},{10,1... | collective-permute-start | bytes 196616 | tf_op jit(solution)/shard_map/ppermute | solution.py:183
  166.4 4.6 %collective-permute-start.4 = (bf16[1,128,256]{2,1,0:T(8,128)(2,1)S(1)}, bf16[1,128,256]{2,1,0:T(8,128)(2,1)S(1)}, u32[]{:S(2)}, u32[]{:S(2)}) collective-permute-start(bf16[1,128,256]{2,1,0:T(8,128)(2,1)S(1)} %collective-permute-done.3), channel_id=1, source_target_pairs={{0,1},{1,2},{2,3},{3,4},{4,5},{5,6},{6,7},{7,0},{8,9},{9,10},{10,1... | collective-permute-start | bytes 196616 | tf_op jit(solution)/shard_map/ppermute | solution.py:183
  170.9 4.6 %collective-permute-start.5 = (bf16[1,128,256]{2,1,0:T(8,128)(2,1)S(1)}, bf16[1,128,256]{2,1,0:T(8,128)(2,1)S(1)}, u32[]{:S(2)}, u32[]{:S(2)}) collective-permute-start(bf16[1,128,256]{2,1,0:T(8,128)(2,1)S(1)} %collective-permute-done.4), channel_id=1, source_target_pairs={{0,1},{1,2},{2,3},{3,4},{4,5},{5,6},{6,7},{7,0},{8,9},{9,10},{10,1... | collective-permute-start | bytes 196616 | tf_op jit(solution)/shard_map/ppermute | solution.py:183
  175.5 4.6 %collective-permute-start.6 = (bf16[1,128,256]{2,1,0:T(8,128)(2,1)S(1)}, bf16[1,128,256]{2,1,0:T(8,128)(2,1)S(1)}, u32[]{:S(2)}, u32[]{:S(2)}) collective-permute-start(bf16[1,128,256]{2,1,0:T(8,128)(2,1)S(1)} %collective-permute-done.5), channel_id=1, source_target_pairs={{0,1},{1,2},{2,3},{3,4},{4,5},{5,6},{6,7},{7,0},{8,9},{9,10},{10,1... | collective-permute-start | bytes 196616 | tf_op jit(solution)/shard_map/ppermute | solution.py:183
  180.1 22.3 %collective-permute-start.7 = (bf16[1,128,256]{2,1,0:T(8,128)(2,1)S(1)}, bf16[1,128,256]{2,1,0:T(8,128)(2,1)S(1)}, u32[]{:S(2)}, u32[]{:S(2)}) collective-permute-start(bf16[1,128,256]{2,1,0:T(8,128)(2,1)S(1)} %collective-permute-done.6), channel_id=1, source_target_pairs={{0,1},{1,2},{2,3},{3,4},{4,5},{5,6},{6,7},{7,0},{8,9},{9,10},{10,1... | collective-permute-start | bytes 196616 | tf_op jit(solution)/shard_map/ppermute | solution.py:183
  198.4 15.1 %all-to-all-start = ((bf16[8,2,20480]{2,1,0:T(2,128)(2,1)}), bf16[8,2,20480]{2,1,0:T(2,128)(2,1)S(1)}, u32[]{:S(2)}, u32[]{:S(2)}) async-start(bf16[8,2,20480]{2,1,0:T(2,128)(2,1)} %reshape.674), calls=%async_computation | async-start | bytes 1310720 | tf_op jit(solution)/shard_map/all_to_all | solution.py:179
